TPU v7x, 512 devices: a whole 4x8x8 slice. The times are simulated.
512 devices in a mesh: grp: 16 (over z, core), dev: 32 (over x, y).
Axes of the slice: x: 4, y: 8, z: 8, core: 2. Of those that a mesh axis runs over, the one named last changes fastest.
Arguments:
- ssm_input: bfloat16 [4096, 4096], P('grp', 'dev'), may hold values from -6 to 6
- gate_input: bfloat16 [4096, 4096], P('grp', 'dev'), may hold values from -6 to 6
- step_size: float32 [4096, 64], P('grp', 'dev'), may hold values from 6.1035156e-05 to 0.3375
- decay_rate: float32 [64], P('dev'), may hold values from 0.5 to 2
- in_coeff: bfloat16 [4096, 128], P('grp'), may hold values from -6 to 6
- out_coeff: bfloat16 [4096, 128], P('grp'), may hold values from -6 to 6
- skip_gain: float32 [64], P('dev'), may hold values from 0.5 to 3
- norm_gain: float32 [4096], P('dev'), may hold values from 0.5 to 1.5
- out_proj: bfloat16 [4096, 2048], P(None, 'dev'), may hold values from -0.09375 to 0.09375
- residual: bfloat16 [4096, 2048], P(('grp', 'dev')), may hold values from -6 to 6
- ffn_gain: float32 [2048], replicated, may hold values from 0.5 to 1.5
- router: float32 [2048, 16], replicated, may hold values from -0.125 to 0.125
- routes: int32 [4096, 2], P(('grp', 'dev')), may hold values from 0 to 15, all different within a row; in each aligned block of 8 rows (0 to 7, 8 to 15, ...) at most 2 rows name the same one
- gate_weight: bfloat16 [16, 2048, 8192], P('grp', None, 'dev'), may hold values from -0.125 to 0.125
- up_weight: bfloat16 [16, 2048, 8192], P('grp', None, 'dev'), may hold values from -0.125 to 0.125
- down_weight: bfloat16 [16, 8192, 2048], P('grp', 'dev'), may hold values from -0.0625 to 0.0625
Outputs:
- moe_out: bfloat16 [4096, 2048], P(('grp', 'dev'))
Inputs may be any that keep to these rules, and one draw needn't show every extreme that they name: `routes`: each row names two different experts; among the 8 rows of one dispatch block of consecutive tokens no expert is named more than 2 times, a bound that some block reaches.
All inputs are finite; a program needn't handle non-finite values.
Results may differ from a plain program's by a relative error of at most 0.012.
Values may be sent and summed in bfloat16 or wider, within the bound.
No kernel may reach another device: no remote copies, remote signals or barrier semaphores. Data moves between devices by JAX's collectives and lax.ppermute only.
A program may use at most 64 MiB of HBM per device.

v0:
```python
import jax
import jax.numpy as jnp
from jax import lax
from jax.sharding import Mesh
from jax.sharding import PartitionSpec as P

DEV = ("dev_0", "dev_1")
GRP_DEV = ("grp", "dev_0", "dev_1")
EPSILON = 1e-05
HIGHEST_PREC = lax.Precision.HIGHEST


def side_by_side(arrays, axis, dim, along):
    columns = [a.reshape(*a.shape[:along], -1) for a in arrays]
    both = jnp.concatenate(columns, axis=along)
    filled, at, finished = (lax.all_gather(both, axis, axis=dim, tiled=True), 0, [])
    for a, column in zip(arrays, columns):
        piece = filled[..., at : at + column.shape[along]]
        finished.append(piece.reshape(*piece.shape[:along], *a.shape[along:]))
        at += column.shape[along]
    return tuple(finished)


def sent_to_all(shard, axis):
    peers = lax.axis_size(axis)
    return lax.all_to_all(
        jnp.broadcast_to(shard[None], (peers, *shard.shape)), axis, 0, 0, tiled=True
    )


def of_everyone(shard, axis):
    everything = sent_to_all(shard, axis)
    return jnp.sum(everything, axis=0)


def in_order(tiles, dim):
    dims = list(tiles.shape[1:])
    dims[dim] *= tiles.shape[0]
    return jnp.moveaxis(tiles, 0, dim).reshape(dims)


def collect(shard, axis, dim):
    return in_order(sent_to_all(shard, axis), dim)


def sum_by_axis(terms, axes):
    total = terms.astype(jnp.bfloat16)
    for axis in axes:
        total = lax.psum_scatter(total, axis, scatter_dimension=0, tiled=True)
    return total.astype(jnp.float32)


def rms_scale(values, gain_vec):
    return (
        values * lax.rsqrt(jnp.mean(values * values, axis=-1, keepdims=True) + EPSILON) * gain_vec
    )


def slot_tables(routes_block, expert_count, slot_cap):
    blocks, row_total = (routes_block.shape[0], routes_block.shape[1])
    flat_routes = routes_block.reshape(blocks, row_total * 2)
    onehot = (
        flat_routes[:, :, None] == jnp.arange(expert_count, dtype=jnp.int32)[None, None, :]
    ).astype(jnp.int32)
    earlier = jnp.cumsum(onehot, axis=1) - onehot
    slot_rank = jnp.sum(earlier * onehot, axis=2)
    slot_index = (flat_routes * slot_cap + slot_rank).reshape(blocks, row_total, 2)
    placed = (
        slot_index[:, :, :, None]
        == jnp.arange(expert_count * slot_cap, dtype=jnp.int32)[None, None, None, :]
    )
    return placed.astype(jnp.float32)


def shards(
    ssm_input,
    gate_input,
    step_size,
    decay_rate,
    in_coeff,
    out_coeff,
    skip_gain,
    norm_gain,
    out_proj,
    residual,
    ffn_gain,
    router,
    routes,
    gate_weight,
    up_weight,
    down_weight,
):
    tok_rows = ssm_input.shape[0]
    head_count = step_size.shape[1]
    head_width = ssm_input.shape[1] // head_count
    dev_count = lax.axis_size(DEV)
    inner_dim = ssm_input.shape[1] * dev_count
    block_rows = residual.shape[0]
    model_dim = residual.shape[1]
    experts = lax.axis_size("grp")
    slot_cap = max(2, 4 * block_rows // experts)
    group_slots = experts * slot_cap
    inputs_f = ssm_input.astype(jnp.float32).reshape(tok_rows, head_count, head_width)
    in_float = in_coeff.astype(jnp.float32)
    out_float = out_coeff.astype(jnp.float32)
    log_rate = -(step_size * decay_rate[None, :])
    cumulative = jnp.cumsum(log_rate, axis=0)
    causal = (jnp.arange(tok_rows)[:, None] >= jnp.arange(tok_rows)[None, :])[:, :, None]
    spread = cumulative[:, None, :] - cumulative[None, :, :]
    decay_pair = jnp.where(causal, jnp.exp(jnp.where(causal, spread, 0.0)), 0.0)
    scores = jnp.dot(out_coeff, in_coeff.T, preferred_element_type=jnp.float32)
    mixing = decay_pair * scores[:, :, None] * step_size[None, :, :]
    inside = jnp.einsum("tuh,uhp->thp", mixing, inputs_f, precision=HIGHEST_PREC)
    to_end = jnp.exp(cumulative[-1][None, :] - cumulative) * step_size
    own_state = jnp.einsum("uh,uhp,un->hpn", to_end, inputs_f, in_float, precision=HIGHEST_PREC)
    own_log = cumulative[-1]
    group_logs, group_states = tuple(
        (
            part.astype(jnp.float32)
            for part in side_by_side(
                (own_log[None].astype(jnp.bfloat16), own_state[None].astype(jnp.bfloat16)),
                "grp",
                0,
                2,
            )
        )
    )
    group_index = jnp.arange(group_logs.shape[0])
    my_group = lax.axis_index("grp")
    inclusive = jnp.cumsum(group_logs, axis=0)
    exclusive = inclusive - group_logs
    before_me = jnp.sum(jnp.where((group_index == my_group)[:, None], exclusive, 0.0), axis=0)
    earlier_mask = (group_index < my_group)[:, None]
    weighting = jnp.where(
        earlier_mask, jnp.exp(jnp.where(earlier_mask, before_me[None, :] - inclusive, 0.0)), 0.0
    )
    entering = jnp.einsum("gh,ghpn->hpn", weighting, group_states, precision=HIGHEST_PREC)
    carried = jnp.exp(cumulative)[:, :, None] * jnp.einsum(
        "hpn,tn->thp", entering, out_float, precision=HIGHEST_PREC
    )
    ssm_out = inside + carried + skip_gain[None, :, None] * inputs_f
    gated_out = ssm_out.reshape(tok_rows, head_count * head_width) * jax.nn.silu(
        gate_input.astype(jnp.float32)
    )
    squares = of_everyone(jnp.sum(gated_out * gated_out, axis=1), DEV)
    mixed_rows = (
        gated_out * lax.rsqrt(squares[:, None] / inner_dim + EPSILON) * norm_gain[None, :]
    ).astype(jnp.bfloat16)
    projected = jnp.dot(
        collect(mixed_rows, DEV, 1), out_proj, preferred_element_type=jnp.float32
    ).astype(jnp.bfloat16)
    mamba_out = lax.all_to_all(projected, DEV, split_axis=0, concat_axis=1, tiled=True)
    hidden_res = (residual.astype(jnp.float32) + mamba_out.astype(jnp.float32)).astype(jnp.bfloat16)
    hidden_float = hidden_res.astype(jnp.float32)
    normed = rms_scale(hidden_float, ffn_gain).astype(jnp.bfloat16)
    logits = jnp.dot(normed.astype(jnp.float32), router, precision=HIGHEST_PREC)
    expert_ids = jnp.arange(experts, dtype=jnp.int32)[None, :]
    first_logit = jnp.sum(logits * (routes[:, 0:1] == expert_ids).astype(jnp.float32), axis=1)
    second_logit = jnp.sum(logits * (routes[:, 1:2] == expert_ids).astype(jnp.float32), axis=1)
    first_prob = jax.nn.sigmoid(first_logit - second_logit)
    second_prob = 1.0 - first_prob
    placed = slot_tables(routes[None], experts, slot_cap)[0]
    filled = jnp.sum(placed, axis=1)
    outgoing = jnp.dot(
        filled.T.astype(jnp.bfloat16), normed, preferred_element_type=jnp.float32
    ).astype(jnp.bfloat16)
    outgoing = outgoing.reshape(experts, slot_cap, model_dim)
    arrived = lax.all_to_all(outgoing, "grp", split_axis=0, concat_axis=0, tiled=True)
    all_rows = lax.all_gather(arrived, DEV, axis=0, tiled=True).reshape(-1, model_dim)
    gate_act = jnp.dot(all_rows, gate_weight[0], preferred_element_type=jnp.float32)
    up_act = jnp.dot(all_rows, up_weight[0], preferred_element_type=jnp.float32)
    hidden = (jax.nn.silu(gate_act) * up_act).astype(jnp.bfloat16)
    summed = sum_by_axis(jnp.dot(hidden, down_weight[0], preferred_element_type=jnp.float32), DEV)
    returned = lax.all_to_all(
        summed.astype(jnp.bfloat16).reshape(experts, slot_cap, model_dim),
        "grp",
        split_axis=0,
        concat_axis=0,
        tiled=True,
    )
    weights = first_prob[:, None] * placed[:, 0, :] + second_prob[:, None] * placed[:, 1, :]
    contrib = jnp.dot(
        weights,
        returned.reshape(group_slots, model_dim).astype(jnp.float32),
        precision=HIGHEST_PREC,
    )
    return (hidden_float + contrib).astype(jnp.bfloat16)


def solution(mesh):
    torus = Mesh(mesh.devices.reshape(mesh.shape["grp"], 4, 8), ("grp", "dev_0", "dev_1"))
    in_specs = (
        P("grp", DEV),
        P("grp", DEV),
        P("grp", DEV),
        P(DEV),
        P("grp", None),
        P("grp", None),
        P(DEV),
        P(DEV),
        P(None, DEV),
        P(GRP_DEV, None),
        P(),
        P(),
        P(GRP_DEV, None),
        P("grp", None, DEV),
        P("grp", None, DEV),
        P("grp", DEV, None),
    )
    out_specs = P(GRP_DEV, None)
    return jax.shard_map(
        shards, mesh=torus, in_specs=in_specs, out_specs=out_specs, check_vma=False
    )
```

profile of v0, /device:TPU:1, one launch (start us, length us, event | category | flops | bytes accessed | tf_op | source)
XLA Modules:
  0.0 366.3 jit_solution(13563389187455256031)
XLA Ops:
  6.6 0.9 negate_bitcast_fusion
  7.4 0.6 reduce-window.6
  8.1 0.2 slice_reduce_fusion
  8.2 0.2 reduce-window.9
  8.5 0.2 slice_reduce_fusion.1
  8.7 0.9 copy.73
  9.7 0.8 fusion.55
  10.4 1.0 convolution_convert_fusion.2
  11.5 0.1 pad_maximum_fusion
  11.6 26.0 %all_gather.6 = bf16[16,2,8193]{2,1,0:T(2,128)(2,1)S(1)} all-gather(bf16[1,2,8193]{2,1,0:T(2,128)(2,1)S(1)} %pad_maximum_fusion), channel_id=1, replica_groups=mesh['grp'=16,'dev_0'=4,'dev_1'=8] {'grp'}, dimensions={0}, use_global_device_ids=true | all-gather | bytes 557124 | tf_op jit(solution)/shard_map/all_gather | solution.py:16
  37.6 0.7 slice.40
  38.3 0.1 copy.90
  38.5 0.1 select_reduce_fusion.1
  38.8 0.4 reshape.245
  39.2 1.1 fusion.56
  40.3 0.5 fusion.15
  40.8 0.2 fusion.4
  41.1 0.6 fusion.3
  41.8 0.1 multiply_reduce_fusion
  42.0 18.2 %all_to_all.34 = f32[32,1,256]{2,1,0:T(1,128)S(1)} all-to-all(f32[32,1,256]{2,1,0:T(1,128)S(1)} %broadcast_in_dim.80), channel_id=1, replica_groups=mesh['grp'=16,'dev_0'=4,'dev_1'=8] {'dev_0','dev_1'}, dimensions={0} | all-to-all | bytes 65536 | tf_op jit(solution)/shard_map/all_to_all | solution.py:26
  60.3 0.1 multiply_convert_fusion
  60.4 0.1 copy.80
  60.5 1.6 broadcast_in_dim.81
  62.1 4.1 %all-to-all-start.1 = ((bf16[32,256,128]{1,2,0:T(8,128)(2,1)}), bf16[32,256,128]{1,2,0:T(8,128)(2,1)S(1)}, u32[]{:S(2)}, u32[]{:S(2)}) async-start(bf16[32,256,128]{1,2,0:T(8,128)(2,1)} %broadcast_in_dim.81), calls=%async_computation.1 | async-start | bytes 4194304 | tf_op jit(solution)/shard_map/all_to_all | solution.py:26
  66.5 0.2 select_reduce_fusion
  66.9 48.6 %all-to-all-done.1 = bf16[32,256,128]{1,2,0:T(8,128)(2,1)S(1)} async-done(((bf16[32,256,128]{1,2,0:T(8,128)(2,1)}), bf16[32,256,128]{1,2,0:T(8,128)(2,1)S(1)}, u32[]{:S(2)}, u32[]{:S(2)}) %all-to-all-start.1) | async-done | bytes 2097184 | tf_op jit(solution)/shard_map/all_to_all | solution.py:26
  115.5 1.5 convolution_convert_fusion.3
  117.0 0.1 copy.81
  117.1 0.7 reshape.260
  117.9 6.4 %all-to-all-start.2 = ((bf16[32,2,256]{2,1,0:T(2,128)(2,1)}), bf16[32,2,256]{2,1,0:T(2,128)(2,1)S(1)}, u32[]{:S(2)}, u32[]{:S(2)}) async-start(bf16[32,2,256]{2,1,0:T(2,128)(2,1)} %reshape.260), calls=%async_computation.2 | async-start | bytes 65536 | tf_op jit(solution)/shard_map/all_to_all | solution.py:152
  124.4 8.6 %all-to-all-done.2 = bf16[32,2,256]{2,1,0:T(2,128)(2,1)S(1)} async-done(((bf16[32,2,256]{2,1,0:T(2,128)(2,1)}), bf16[32,2,256]{2,1,0:T(2,128)(2,1)S(1)}, u32[]{:S(2)}, u32[]{:S(2)}) %all-to-all-start.2) | async-done | bytes 32800 | tf_op jit(solution)/shard_map/all_to_all | solution.py:152
  133.1 0.1 reshape.261
  133.2 0.1 reshape.253
  133.3 0.1 fusion.34
  133.5 0.2 convolution_convert_fusion.1
  133.7 0.1 reshape.248
  133.8 14.9 %all_to_all.35 = bf16[16,2,2048]{2,1,0:T(2,128)(2,1)} all-to-all(bf16[16,2,2048]{2,1,0:T(2,128)(2,1)S(1)} %reshape.248), channel_id=1, replica_groups=mesh['grp'=16,'dev_0'=4,'dev_1'=8] {'grp'}, dimensions={0} | all-to-all | bytes 262144 | tf_op jit(solution)/shard_map/all_to_all | solution.py:168
  148.8 73.9 %all-gather.2.cloned.1.call-done = bf16[512,2,2048]{2,1,0:T(2,128)(2,1)} async-done(((bf16[16,2,2048]{2,1,0:T(2,128)(2,1)}), bf16[512,2,2048]{2,1,0:T(2,128)(2,1)}) %all-gather.2.cloned.1.call-update) | async-done | bytes 4194320 | tf_op jit(solution)/shard_map/all_gather | solution.py:169
  222.7 7.2 %reshape.249 = bf16[1024,2048]{1,0:T(8,128)(2,1)} reshape(bf16[512,2,2048]{2,1,0:T(2,128)(2,1)} %all-gather.2.cloned.1.call-done) | data formatting | bytes 8388608 | tf_op jit(solution)/shard_map/reshape | solution.py:169
  229.9 4.5 %fusion.8 = f32[1024,256]{1,0:T(8,128)} fusion(bf16[1024,2048]{1,0:T(8,128)(2,1)} %reshape.249, bf16[1,2048,256]{2,1,0:T(8,128)(2,1)S(1)} %copy-done.8), kind=kOutput, calls=%fused_computation.15 | convolution fusion | flops 1073741824 | bytes 6291456 | tf_op jit(solution)/shard_map/dot_general | solution.py:170
  234.4 9.1 %convolution_convert_fusion = bf16[1024,2048]{1,0:T(8,128)(2,1)} fusion(bf16[1024,2048]{1,0:T(8,128)(2,1)} %reshape.249, bf16[1,256,2048]{2,1,0:T(8,128)(2,1)S(1)} %copy-done, bf16[1,2048,256]{2,1,0:T(8,128)(2,1)} %param.30, f32[1024,256]{1,0:T(8,128)} %fusion.8), kind=kOutput, calls=%fused_computation | convolution fusion | flops 2151153664 | bytes 11534336 | tf_op jit(solution)/shard_map/dot_general | solution.py:173
  243.6 52.5 %reduce-scatter.3.cloned.1.call-done = bf16[256,2048]{1,0:T(8,128)(2,1)} async-done(((bf16[1024,2048]{1,0:T(8,128)(2,1)}), bf16[256,2048]{1,0:T(8,128)(2,1)}) %reduce-scatter.3.cloned.1.call-update) | async-done | bytes 1048592 | tf_op jit(solution)/shard_map/reduce_scatter | solution.py:49
  296.2 39.4 %reduce-scatter.5.cloned.1.call-done = bf16[32,2048]{1,0:T(8,128)(2,1)} async-done(((bf16[256,2048]{1,0:T(8,128)(2,1)}), bf16[32,2048]{1,0:T(8,128)(2,1)}) %reduce-scatter.5.cloned.1.call-update) | async-done | bytes 131088 | tf_op jit(solution)/shard_map/reduce_scatter | solution.py:49
  335.6 1.6 reshape.250
  337.2 12.5 %all-to-all-start.4 = ((bf16[16,2,2048]{2,1,0:T(2,128)(2,1)}), bf16[16,2,2048]{2,1,0:T(2,128)(2,1)S(1)}, u32[]{:S(2)}, u32[]{:S(2)}) async-start(bf16[16,2,2048]{2,1,0:T(2,128)(2,1)} %reshape.250), calls=%async_computation.6 | async-start | bytes 262144 | tf_op jit(solution)/shard_map/all_to_all | solution.py:174
  349.7 0.3 select_reduce_fusion.2
  350.1 8.8 %all-to-all-done.4 = bf16[16,2,2048]{2,1,0:T(2,128)(2,1)S(1)} async-done(((bf16[16,2,2048]{2,1,0:T(2,128)(2,1)}), bf16[16,2,2048]{2,1,0:T(2,128)(2,1)S(1)}, u32[]{:S(2)}, u32[]{:S(2)}) %all-to-all-start.4) | async-done | bytes 131104 | tf_op jit(solution)/shard_map/all_to_all | solution.py:174
  358.9 0.9 fusion
  (60 shorter events, 1.6 us)
Async XLA Ops:
  6.5 227.9 %copy-start = (bf16[1,256,2048]{2,1,0:T(8,128)(2,1)S(1)}, bf16[1,256,2048]{2,1,0:T(8,128)(2,1)}, u32[]{:S(2)}) copy-start(bf16[1,256,2048]{2,1,0:T(8,128)(2,1)} %param.31) | copy-start | bytes 3145732
  6.5 34.5 %copy-start.5 = (f32[256,2]{0,1:T(2,128)S(1)}, f32[256,2]{0,1:T(2,128)}, u32[]{:S(2)}) copy-start(f32[256,2]{0,1:T(2,128)} %param.18) | copy-start | bytes 6148
  6.5 34.3 %copy-start.2 = (bf16[256,128]{1,0:T(8,128)(2,1)S(1)}, bf16[256,128]{1,0:T(8,128)(2,1)}, u32[]{:S(2)}) copy-start(bf16[256,128]{1,0:T(8,128)(2,1)} %param.21) | copy-start | bytes 196612
  6.5 34.5 %copy-start.10 = (f32[2]{0:T(128)S(1)}, f32[2]{0:T(128)}, u32[]{:S(2)}) copy-start(f32[2]{0:T(128)} %param.22) | copy-start | bytes 28
  6.5 35.3 %copy-start.1 = (bf16[256,128]{1,0:T(8,128)(2,1)S(1)}, bf16[256,128]{1,0:T(8,128)(2,1)}, u32[]{:S(2)}) copy-start(bf16[256,128]{1,0:T(8,128)(2,1)} %param.17) | copy-start | bytes 196612
  6.5 53.7 %copy-start.7 = (f32[128]{0:T(128)S(1)}, f32[128]{0:T(128)}, u32[]{:S(2)}) copy-start(f32[128]{0:T(128)} %param.23) | copy-start | bytes 1540
  41.1 25.2 %copy-start.6 = (s32[8,2]{0,1:T(2,128)S(1)}, s32[8,2]{0,1:T(2,128)}, u32[]{:S(2)}) copy-start(s32[8,2]{0,1:T(2,128)} %param.28) | copy-start | bytes 196
  62.1 71.2 %copy-start.3 = (bf16[8,2048]{1,0:T(8,128)(2,1)S(1)}, bf16[8,2048]{1,0:T(8,128)(2,1)}, u32[]{:S(2)}) copy-start(bf16[8,2048]{1,0:T(8,128)(2,1)} %param.25) | copy-start | bytes 98308
  62.1 71.4 %copy-start.4 = (f32[2048]{0:T(1024)S(1)}, f32[2048]{0:T(1024)}, u32[]{:S(2)}) copy-start(f32[2048]{0:T(1024)} %param.26) | copy-start | bytes 24580
  62.1 53.4 %all-to-all-start.1 = ((bf16[32,256,128]{1,2,0:T(8,128)(2,1)}), bf16[32,256,128]{1,2,0:T(8,128)(2,1)S(1)}, u32[]{:S(2)}, u32[]{:S(2)}) async-start(bf16[32,256,128]{1,2,0:T(8,128)(2,1)} %broadcast_in_dim.81), calls=%async_computation.1 | async-start | bytes 4194304 | tf_op jit(solution)/shard_map/all_to_all | solution.py:26
  117.9 15.2 %all-to-all-start.2 = ((bf16[32,2,256]{2,1,0:T(2,128)(2,1)}), bf16[32,2,256]{2,1,0:T(2,128)(2,1)S(1)}, u32[]{:S(2)}, u32[]{:S(2)}) async-start(bf16[32,2,256]{2,1,0:T(2,128)(2,1)} %reshape.260), calls=%async_computation.2 | async-start | bytes 65536 | tf_op jit(solution)/shard_map/all_to_all | solution.py:152
  124.3 98.4 %all-gather.2.cloned.1.call-start = ((), (), s32[]{:S(2)}) async-start(), calls=%async_computation.7 | async-start | bytes 4325376 | tf_op jit(solution)/shard_map/all_gather | solution.py:169
  148.8 81.2 %copy-start.8 = (bf16[1,2048,256]{2,1,0:T(8,128)(2,1)S(1)}, bf16[1,2048,256]{2,1,0:T(8,128)(2,1)}, u32[]{:S(2)}) copy-start(bf16[1,2048,256]{2,1,0:T(8,128)(2,1)} %param.29) | copy-start | bytes 3145732
  148.8 147.3 %reduce-scatter.3.cloned.1.call-start = ((), (), s32[]{:S(2)}) async-start(), calls=%async_computation.8 | async-start | bytes 5242880 | tf_op jit(solution)/shard_map/reduce_scatter | solution.py:49
  243.5 106.1 %copy-start.9 = (f32[2048,16]{0,1:T(8,128)S(1)}, f32[2048,16]{0,1:T(8,128)}, u32[]{:S(2)}) copy-start(f32[2048,16]{0,1:T(8,128)} %param.27) | copy-start | bytes 393220
  243.6 92.0 %reduce-scatter.5.cloned.1.call-start = ((), (), s32[]{:S(2)}) async-start(), calls=%async_computation.9 | async-start | bytes 1179648 | tf_op jit(solution)/shard_map/reduce_scatter | solution.py:49
  337.2 21.6 %all-to-all-start.4 = ((bf16[16,2,2048]{2,1,0:T(2,128)(2,1)}), bf16[16,2,2048]{2,1,0:T(2,128)(2,1)S(1)}, u32[]{:S(2)}, u32[]{:S(2)}) async-start(bf16[16,2,2048]{2,1,0:T(2,128)(2,1)} %reshape.250), calls=%async_computation.6 | async-start | bytes 262144 | tf_op jit(solution)/shard_map/all_to_all | solution.py:174
Sparse Core Ops, SparseCore 0:
  148.9 73.7 all-gather.1
  243.7 52.3 reduce-scatter.2
  299.1 36.3 reduce-scatter.4
where the time goes:
time: 367 us; the launch traced here: 366 us
  waiting for transfers between devices  232 us (63%)
  blocking collectives  59.1 us (16%)
  starting transfers between devices  23.1 us (6%)
  matrix products  20.1 us (5%)
  local copies, waits for them, and re-layouts  15 us (4%)
  between operations  13.4 us (4%)
  other arithmetic  3.74 us (1%)
    reduce_scatter x2, waiting for transfers between devices, sum_by_axis(): total = lax.psum_scatter(total, axis, scatter_dimension=0, tiled=True)  91.8 us
    all_gather x1, waiting for transfers between devices, shards(): lax.all_gather(arrived, DEV, axis=0, tiled=True).reshape(-1, model_dim)  73.9 us
    all_to_all x1, waiting for transfers between devices, sent_to_all(): lax.all_to_all(jnp.broadcast_to(shard[None], (peers, *shard.shape)), axis...  48.6 us
    all_gather x1, blocking collectives, side_by_side(): lax.all_gather(both, axis, axis=dim, tiled=True)  26 us
    all_to_all x1, blocking collectives, sent_to_all(): lax.all_to_all(jnp.broadcast_to(shard[None], (peers, *shard.shape)), axis...  18.2 us
    all_to_all x1, blocking collectives, shards(): lax.all_to_all(outgoing, 'grp', split_axis=0, concat_axis=0, tiled=True)  14.9 us
    all_to_all x1, starting transfers between devices, shards(): lax.all_to_all(summed.astype(jnp.bfloat16).reshape(experts, slot_cap, mod...  12.5 us
    dot_general x1, matrix products, shards(): jnp.dot(hidden, down_weight[0], preferred_element_type=jnp.float32)  9.1 us
  transfers between devices with their start and end apart: 6, of which 6 were waited for; matrix products, arithmetic and copies ran while one was open for 0% of the time, Pallas kernels for 0%

commit v1 on v0

--- a/solution.py
+++ b/solution.py
@@ -149,7 +149,15 @@
     projected = jnp.dot(
         collect(mixed_rows, DEV, 1), out_proj, preferred_element_type=jnp.float32
     ).astype(jnp.bfloat16)
-    mamba_out = lax.all_to_all(projected, DEV, split_axis=0, concat_axis=1, tiled=True)
+    mamba_out = jnp.concatenate(
+        jax.lax.all_to_all(
+            jnp.stack(jnp.split(projected, jax.lax.axis_size(DEV), 0), 0),
+            split_axis=0,
+            axis_name=DEV,
+            concat_axis=0,
+        ),
+        1,
+    )
     hidden_res = (residual.astype(jnp.float32) + mamba_out.astype(jnp.float32)).astype(jnp.bfloat16)
     hidden_float = hidden_res.astype(jnp.float32)
     normed = rms_scale(hidden_float, ffn_gain).astype(jnp.bfloat16)

time: 367 us -> 370 us (level)
  no operation moved by 1% of the time
where the time goes in v1:
time: 370 us; the launch traced here: 369 us
  waiting for transfers between devices  232 us (63%)
  blocking collectives  59.1 us (16%)
  starting transfers between devices  23.3 us (6%)
  matrix products  20.1 us (5%)
  local copies, waits for them, and re-layouts  18.1 us (5%)
  between operations  13.5 us (4%)
  other arithmetic  3.74 us (1%)
    reduce_scatter x2, waiting for transfers between devices, sum_by_axis(): total = lax.psum_scatter(total, axis, scatter_dimension=0, tiled=True)  91.9 us
    all_gather x1, waiting for transfers between devices, shards(): lax.all_gather(arrived, DEV, axis=0, tiled=True).reshape(-1, model_dim)  73.7 us
    all_to_all x1, waiting for transfers between devices, sent_to_all(): lax.all_to_all(jnp.broadcast_to(shard[None], (peers, *shard.shape)), axis...  48.6 us
    all_gather x1, blocking collectives, side_by_side(): lax.all_gather(both, axis, axis=dim, tiled=True)  26 us
    all_to_all x1, blocking collectives, sent_to_all(): lax.all_to_all(jnp.broadcast_to(shard[None], (peers, *shard.shape)), axis...  18.2 us
    all_to_all x1, blocking collectives, shards(): lax.all_to_all(outgoing, 'grp', split_axis=0, concat_axis=0, tiled=True)  14.9 us
    all_to_all x1, starting transfers between devices, shards(): lax.all_to_all(summed.astype(jnp.bfloat16).reshape(experts, slot_cap, mod...  12.4 us
    dot_general x1, matrix products, shards(): jnp.dot(hidden, down_weight[0], preferred_element_type=jnp.float32)  9.1 us
  transfers between devices with their start and end apart: 6, of which 6 were waited for; matrix products, arithmetic and copies ran while one was open for 0% of the time, Pallas kernels for 0%

profile of v1, /device:TPU:1, one launch (start us, length us, event | category | flops | bytes accessed | tf_op | source)
XLA Modules:
  0.0 369.5 jit_solution(9041834502989573428)
XLA Ops:
  6.6 0.9 negate_bitcast_fusion
  7.4 0.6 reduce-window.6
  8.1 0.2 slice_reduce_fusion
  8.2 0.2 reduce-window.9
  8.5 0.2 slice_reduce_fusion.1
  8.7 0.9 copy.165
  9.7 0.8 fusion.55
  10.4 1.0 convolution_convert_fusion.2
  11.5 0.1 pad_maximum_fusion
  11.6 26.0 %all_gather.6 = bf16[16,2,8193]{2,1,0:T(2,128)(2,1)S(1)} all-gather(bf16[1,2,8193]{2,1,0:T(2,128)(2,1)S(1)} %pad_maximum_fusion), channel_id=1, replica_groups=mesh['grp'=16,'dev_0'=4,'dev_1'=8] {'grp'}, dimensions={0}, use_global_device_ids=true | all-gather | bytes 557124 | tf_op jit(solution)/shard_map/all_gather | solution.py:16
  37.6 0.7 slice.40
  38.3 0.1 copy.213
  38.8 0.4 reshape.244
  39.2 1.1 fusion.56
  40.3 0.6 fusion.15
  40.8 0.2 fusion.4
  41.1 0.6 fusion.3
  41.8 0.1 multiply_reduce_fusion
  42.0 18.2 %all_to_all.26 = f32[32,1,256]{2,1,0:T(1,128)S(1)} all-to-all(f32[32,1,256]{2,1,0:T(1,128)S(1)} %broadcast_in_dim.80), channel_id=1, replica_groups=mesh['grp'=16,'dev_0'=4,'dev_1'=8] {'dev_0','dev_1'}, dimensions={0} | all-to-all | bytes 65536 | tf_op jit(solution)/shard_map/all_to_all | solution.py:26
  60.3 0.1 multiply_convert_fusion
  60.4 0.1 copy.172
  60.5 1.6 broadcast_in_dim.81
  62.1 4.1 %all-to-all-start.1 = ((bf16[32,256,128]{1,2,0:T(8,128)(2,1)}), bf16[32,256,128]{1,2,0:T(8,128)(2,1)S(1)}, u32[]{:S(2)}, u32[]{:S(2)}) async-start(bf16[32,256,128]{1,2,0:T(8,128)(2,1)} %broadcast_in_dim.81), calls=%async_computation.1 | async-start | bytes 4194304 | tf_op jit(solution)/shard_map/all_to_all | solution.py:26
  66.5 0.2 select_reduce_fusion
  66.9 48.6 %all-to-all-done.1 = bf16[32,256,128]{1,2,0:T(8,128)(2,1)S(1)} async-done(((bf16[32,256,128]{1,2,0:T(8,128)(2,1)}), bf16[32,256,128]{1,2,0:T(8,128)(2,1)S(1)}, u32[]{:S(2)}, u32[]{:S(2)}) %all-to-all-start.1) | async-done | bytes 2097184 | tf_op jit(solution)/shard_map/all_to_all | solution.py:26
  115.5 1.5 convolution_convert_fusion.3
  117.0 0.1 slice_bitcast_fusion.19
  117.1 0.2 slice_bitcast_fusion
  120.3 0.7 reshape.259
  121.1 6.4 %all-to-all-start.2 = ((bf16[32,2,256]{2,1,0:T(2,128)(2,1)}), bf16[32,2,256]{2,1,0:T(2,128)(2,1)S(1)}, u32[]{:S(2)}, u32[]{:S(2)}) async-start(bf16[32,2,256]{2,1,0:T(2,128)(2,1)} %reshape.259), calls=%async_computation.2 | async-start | bytes 65536 | tf_op jit(solution)/shard_map/all_to_all | solution.py:153
  127.6 8.6 %all-to-all-done.2 = bf16[32,2,256]{2,1,0:T(2,128)(2,1)S(1)} async-done(((bf16[32,2,256]{2,1,0:T(2,128)(2,1)}), bf16[32,2,256]{2,1,0:T(2,128)(2,1)S(1)}, u32[]{:S(2)}, u32[]{:S(2)}) %all-to-all-start.2) | async-done | bytes 32800 | tf_op jit(solution)/shard_map/all_to_all | solution.py:153
  136.2 0.1 reshape.260
  136.5 0.1 fusion.34
  136.7 0.2 convolution_convert_fusion.1
  136.9 0.1 reshape.247
  137.0 14.9 %all_to_all.27 = bf16[16,2,2048]{2,1,0:T(2,128)(2,1)} all-to-all(bf16[16,2,2048]{2,1,0:T(2,128)(2,1)S(1)} %reshape.247), channel_id=1, replica_groups=mesh['grp'=16,'dev_0'=4,'dev_1'=8] {'grp'}, dimensions={0} | all-to-all | bytes 262144 | tf_op jit(solution)/shard_map/all_to_all | solution.py:176
  152.0 0.2 reduce-scatter.3.cloned.1.call-start
  152.2 73.7 %all-gather.2.cloned.1.call-done = bf16[512,2,2048]{2,1,0:T(2,128)(2,1)} async-done(((bf16[16,2,2048]{2,1,0:T(2,128)(2,1)}), bf16[512,2,2048]{2,1,0:T(2,128)(2,1)}) %all-gather.2.cloned.1.call-update) | async-done | bytes 4194320 | tf_op jit(solution)/shard_map/all_gather | solution.py:177
  225.9 7.2 %reshape.248 = bf16[1024,2048]{1,0:T(8,128)(2,1)} reshape(bf16[512,2,2048]{2,1,0:T(2,128)(2,1)} %all-gather.2.cloned.1.call-done) | data formatting | bytes 8388608 | tf_op jit(solution)/shard_map/reshape | solution.py:177
  233.1 4.5 %fusion.8 = f32[1024,256]{1,0:T(8,128)} fusion(bf16[1024,2048]{1,0:T(8,128)(2,1)} %reshape.248, bf16[1,2048,256]{2,1,0:T(8,128)(2,1)S(1)} %copy-done.8), kind=kOutput, calls=%fused_computation.15 | convolution fusion | flops 1073741824 | bytes 6291456 | tf_op jit(solution)/shard_map/dot_general | solution.py:178
  237.6 9.1 %convolution_convert_fusion = bf16[1024,2048]{1,0:T(8,128)(2,1)} fusion(bf16[1024,2048]{1,0:T(8,128)(2,1)} %reshape.248, bf16[1,256,2048]{2,1,0:T(8,128)(2,1)S(1)} %copy-done, bf16[1,2048,256]{2,1,0:T(8,128)(2,1)} %param.30, f32[1024,256]{1,0:T(8,128)} %fusion.8), kind=kOutput, calls=%fused_computation | convolution fusion | flops 2151153664 | bytes 11534336 | tf_op jit(solution)/shard_map/dot_general | solution.py:181
  246.8 52.5 %reduce-scatter.3.cloned.1.call-done = bf16[256,2048]{1,0:T(8,128)(2,1)} async-done(((bf16[1024,2048]{1,0:T(8,128)(2,1)}), bf16[256,2048]{1,0:T(8,128)(2,1)}) %reduce-scatter.3.cloned.1.call-update) | async-done | bytes 1048592 | tf_op jit(solution)/shard_map/reduce_scatter | solution.py:49
  299.4 39.4 %reduce-scatter.5.cloned.1.call-done = bf16[32,2048]{1,0:T(8,128)(2,1)} async-done(((bf16[256,2048]{1,0:T(8,128)(2,1)}), bf16[32,2048]{1,0:T(8,128)(2,1)}) %reduce-scatter.5.cloned.1.call-update) | async-done | bytes 131088 | tf_op jit(solution)/shard_map/reduce_scatter | solution.py:49
  338.8 1.6 reshape.249
  340.4 12.4 %all-to-all-start.4 = ((bf16[16,2,2048]{2,1,0:T(2,128)(2,1)}), bf16[16,2,2048]{2,1,0:T(2,128)(2,1)S(1)}, u32[]{:S(2)}, u32[]{:S(2)}) async-start(bf16[16,2,2048]{2,1,0:T(2,128)(2,1)} %reshape.249), calls=%async_computation.6 | async-start | bytes 262144 | tf_op jit(solution)/shard_map/all_to_all | solution.py:182
  352.9 0.3 select_reduce_fusion.2
  353.2 8.8 %all-to-all-done.4 = bf16[16,2,2048]{2,1,0:T(2,128)(2,1)S(1)} async-done(((bf16[16,2,2048]{2,1,0:T(2,128)(2,1)}), bf16[16,2,2048]{2,1,0:T(2,128)(2,1)S(1)}, u32[]{:S(2)}, u32[]{:S(2)}) %all-to-all-start.4) | async-done | bytes 131104 | tf_op jit(solution)/shard_map/all_to_all | solution.py:182
  362.1 0.9 fusion
  (125 shorter events, 4.7 us)
Async XLA Ops:
  6.5 231.1 %copy-start = (bf16[1,256,2048]{2,1,0:T(8,128)(2,1)S(1)}, bf16[1,256,2048]{2,1,0:T(8,128)(2,1)}, u32[]{:S(2)}) copy-start(bf16[1,256,2048]{2,1,0:T(8,128)(2,1)} %param.31) | copy-start | bytes 3145732
  6.5 34.5 %copy-start.5 = (f32[256,2]{0,1:T(2,128)S(1)}, f32[256,2]{0,1:T(2,128)}, u32[]{:S(2)}) copy-start(f32[256,2]{0,1:T(2,128)} %param.18) | copy-start | bytes 6148
  6.5 34.3 %copy-start.2 = (bf16[256,128]{1,0:T(8,128)(2,1)S(1)}, bf16[256,128]{1,0:T(8,128)(2,1)}, u32[]{:S(2)}) copy-start(bf16[256,128]{1,0:T(8,128)(2,1)} %param.21) | copy-start | bytes 196612
  6.5 34.5 %copy-start.10 = (f32[2]{0:T(128)S(1)}, f32[2]{0:T(128)}, u32[]{:S(2)}) copy-start(f32[2]{0:T(128)} %param.22) | copy-start | bytes 28
  6.5 35.3 %copy-start.1 = (bf16[256,128]{1,0:T(8,128)(2,1)S(1)}, bf16[256,128]{1,0:T(8,128)(2,1)}, u32[]{:S(2)}) copy-start(bf16[256,128]{1,0:T(8,128)(2,1)} %param.17) | copy-start | bytes 196612
  6.5 53.7 %copy-start.7 = (f32[128]{0:T(128)S(1)}, f32[128]{0:T(128)}, u32[]{:S(2)}) copy-start(f32[128]{0:T(128)} %param.23) | copy-start | bytes 1540
  41.1 25.2 %copy-start.6 = (s32[8,2]{0,1:T(2,128)S(1)}, s32[8,2]{0,1:T(2,128)}, u32[]{:S(2)}) copy-start(s32[8,2]{0,1:T(2,128)} %param.28) | copy-start | bytes 196
  62.1 74.4 %copy-start.3 = (bf16[8,2048]{1,0:T(8,128)(2,1)S(1)}, bf16[8,2048]{1,0:T(8,128)(2,1)}, u32[]{:S(2)}) copy-start(bf16[8,2048]{1,0:T(8,128)(2,1)} %param.25) | copy-start | bytes 98308
  62.1 74.6 %copy-start.4 = (f32[2048]{0:T(1024)S(1)}, f32[2048]{0:T(1024)}, u32[]{:S(2)}) copy-start(f32[2048]{0:T(1024)} %param.26) | copy-start | bytes 24580
  62.1 53.4 %all-to-all-start.1 = ((bf16[32,256,128]{1,2,0:T(8,128)(2,1)}), bf16[32,256,128]{1,2,0:T(8,128)(2,1)S(1)}, u32[]{:S(2)}, u32[]{:S(2)}) async-start(bf16[32,256,128]{1,2,0:T(8,128)(2,1)} %broadcast_in_dim.81), calls=%async_computation.1 | async-start | bytes 4194304 | tf_op jit(solution)/shard_map/all_to_all | solution.py:26
  121.1 15.2 %all-to-all-start.2 = ((bf16[32,2,256]{2,1,0:T(2,128)(2,1)}), bf16[32,2,256]{2,1,0:T(2,128)(2,1)S(1)}, u32[]{:S(2)}, u32[]{:S(2)}) async-start(bf16[32,2,256]{2,1,0:T(2,128)(2,1)} %reshape.259), calls=%async_computation.2 | async-start | bytes 65536 | tf_op jit(solution)/shard_map/all_to_all | solution.py:153
  127.5 98.4 %all-gather.2.cloned.1.call-start = ((), (), s32[]{:S(2)}) async-start(), calls=%async_computation.7 | async-start | bytes 4325376 | tf_op jit(solution)/shard_map/all_gather | solution.py:177
  152.0 81.2 %copy-start.8 = (bf16[1,2048,256]{2,1,0:T(8,128)(2,1)S(1)}, bf16[1,2048,256]{2,1,0:T(8,128)(2,1)}, u32[]{:S(2)}) copy-start(bf16[1,2048,256]{2,1,0:T(8,128)(2,1)} %param.29) | copy-start | bytes 3145732
  152.0 147.3 %reduce-scatter.3.cloned.1.call-start = ((), (), s32[]{:S(2)}) async-start(), calls=%async_computation.8 | async-start | bytes 5242880 | tf_op jit(solution)/shard_map/reduce_scatter | solution.py:49
  246.7 106.1 %copy-start.9 = (f32[2048,16]{0,1:T(8,128)S(1)}, f32[2048,16]{0,1:T(8,128)}, u32[]{:S(2)}) copy-start(f32[2048,16]{0,1:T(8,128)} %param.27) | copy-start | bytes 393220
  246.8 92.0 %reduce-scatter.5.cloned.1.call-start = ((), (), s32[]{:S(2)}) async-start(), calls=%async_computation.9 | async-start | bytes 1179648 | tf_op jit(solution)/shard_map/reduce_scatter | solution.py:49
  340.4 21.6 %all-to-all-start.4 = ((bf16[16,2,2048]{2,1,0:T(2,128)(2,1)}), bf16[16,2,2048]{2,1,0:T(2,128)(2,1)S(1)}, u32[]{:S(2)}, u32[]{:S(2)}) async-start(bf16[16,2,2048]{2,1,0:T(2,128)(2,1)} %reshape.249), calls=%async_computation.6 | async-start | bytes 262144 | tf_op jit(solution)/shard_map/all_to_all | solution.py:182
Sparse Core Ops, SparseCore 0:
  152.1 73.7 all-gather.1
  246.9 52.3 reduce-scatter.2
  302.4 36.3 reduce-scatter.4
